TPU v7x, 512 devices: a whole 4x8x8 slice. The times are simulated.
512 devices in a mesh: pipe: 4 (over z_hi), ctx: 32 (over y, z_lo, core), dp: 4 (over x).
Axes of the slice: x: 4, y: 8, z: 8 (z_hi: 4, z_lo: 2; z = z_hi * 2 + z_lo), core: 2. Of those that a mesh axis runs over, the one named last changes fastest.
Arguments:
- queries: bfloat16 [4, 4, 4096, 4096], P('pipe', 'dp', 'ctx'), may hold values from -7 to 7
- key_input: bfloat16 [4, 4, 4096, 512], P('pipe', 'dp', 'ctx'), may hold values from -4 to 4
- value_input: bfloat16 [4, 4, 4096, 512], P('pipe', 'dp', 'ctx'), may hold values from -6 to 6
- incoming: bfloat16 [4, 4, 4096, 4096], P('pipe', 'dp', 'ctx'), may hold values from -6 to 6
- segments: int32 [4, 4096], P('dp'), may hold values from 0 to 15, never falling along the last dimension, each value on 1 to 512 neighbouring positions
Outputs:
- query_grad: bfloat16 [4, 4, 4096, 4096], P('pipe', 'dp', 'ctx')
- key_grad: bfloat16 [4, 4, 4096, 512], P('pipe', 'dp', 'ctx')
- value_grad: bfloat16 [4, 4, 4096, 512], P('pipe', 'dp', 'ctx')
- bias_grad: float32 [4, 5120], P('pipe')
Inputs may be any that keep to these rules, and one draw needn't show every extreme that they name: `segments`: tokens of one document are contiguous; every document holds 1 to 512 tokens and one holds exactly 512.
All inputs are finite; a program needn't handle non-finite values.
Results may differ from a plain program's by a relative error of at most 0.009.
Values may be sent and summed in bfloat16 or wider, within the bound.
No kernel may reach another device: no remote copies, remote signals or barrier semaphores. Data moves between devices by JAX's collectives and lax.ppermute only.
A program may use at most 64 MiB of HBM per device.

v0:
```python
import math
import jax
import jax.numpy as jnp
from jax import lax
from jax.sharding import PartitionSpec as P

ASKER_STREAMS = 32
SHARED_GROUPS = 4
FEATURE_SIZE = 128
QUERY_PER_KEY = 8


def passed_along(value, axis, steps):
    count = lax.axis_size(axis)
    pairs = [(source, (source + steps) % count) for source in range(count)]
    return lax.ppermute(value, axis, pairs)


def attend(
    queries, key_rows, value_rows, cotangent, query_doc, key_doc, query_pos, key_pos, scaling
):
    scores = (
        jnp.einsum("gqd,kd->gqk", queries, key_rows, preferred_element_type=jnp.float32) * scaling
    )
    visible = (query_doc[:, None] == key_doc[None, :]) & (key_pos[None, :] <= query_pos[:, None])
    scores = jnp.where(visible[None], scores, -1e30)
    row_max = jnp.max(scores, axis=-1, keepdims=True)
    weights = jnp.where(visible[None], jnp.exp(scores - row_max), 0.0)
    probs = weights / jnp.sum(weights, axis=-1, keepdims=True)
    probs_b = probs.astype(jnp.bfloat16)
    attn_out = jnp.einsum("gqk,kd->gqd", probs_b, value_rows, preferred_element_type=jnp.float32)
    dot_out = jnp.sum(cotangent.astype(jnp.float32) * attn_out, axis=-1, keepdims=True)
    grad_prob = jnp.einsum("gqd,kd->gqk", cotangent, value_rows, preferred_element_type=jnp.float32)
    grad_score = (probs * (grad_prob - dot_out) * scaling).astype(jnp.bfloat16)
    asker_derivative = jnp.einsum(
        "gqk,kd->gqd", grad_score, key_rows, preferred_element_type=jnp.float32
    )
    lookup_derivative = jnp.einsum(
        "gqk,gqd->kd", grad_score, queries, preferred_element_type=jnp.float32
    )
    content_derivative = jnp.einsum(
        "gqk,gqd->kd", probs_b, cotangent, preferred_element_type=jnp.float32
    )
    return (asker_derivative, lookup_derivative, content_derivative)


def banded(queries, key_rows, value_rows, cotangent, doc_ids, block_len, scaling):
    length = doc_ids.shape[0]
    blocks = length // block_len
    width = key_rows.shape[1]
    key_pad = jnp.concatenate([jnp.zeros((block_len, width), key_rows.dtype), key_rows], axis=0)
    value_pad = jnp.concatenate(
        [jnp.zeros((block_len, width), value_rows.dtype), value_rows], axis=0
    )
    doc_pad = jnp.concatenate([jnp.full((block_len,), -1, jnp.int32), doc_ids])
    pos_pad = jnp.arange(length + block_len, dtype=jnp.int32) - block_len

    def step(carried, block):
        key_acc, value_acc = carried
        anchor = block * block_len
        query_blk = lax.dynamic_slice_in_dim(queries, anchor, block_len, 1)
        cot_blk = lax.dynamic_slice_in_dim(cotangent, anchor, block_len, 1)
        key_blk = lax.dynamic_slice_in_dim(key_pad, anchor, 2 * block_len, 0)
        value_blk = lax.dynamic_slice_in_dim(value_pad, anchor, 2 * block_len, 0)
        query_doc = lax.dynamic_slice_in_dim(doc_ids, anchor, block_len, 0)
        key_doc = lax.dynamic_slice_in_dim(doc_pad, anchor, 2 * block_len, 0)
        query_pos = anchor + jnp.arange(block_len, dtype=jnp.int32)
        key_pos = lax.dynamic_slice_in_dim(pos_pad, anchor, 2 * block_len, 0)
        asker_derivative, lookup_derivative, content_derivative = attend(
            query_blk, key_blk, value_blk, cot_blk, query_doc, key_doc, query_pos, key_pos, scaling
        )
        key_acc = lax.dynamic_update_slice_in_dim(
            key_acc,
            lax.dynamic_slice_in_dim(key_acc, anchor, 2 * block_len, 0) + lookup_derivative,
            anchor,
            0,
        )
        value_acc = lax.dynamic_update_slice_in_dim(
            value_acc,
            lax.dynamic_slice_in_dim(value_acc, anchor, 2 * block_len, 0) + content_derivative,
            anchor,
            0,
        )
        return ((key_acc, value_acc), asker_derivative)

    start_acc = jnp.zeros((length + block_len, width), jnp.float32)
    (key_acc, value_acc), query_blocks = lax.scan(
        step, (start_acc, start_acc), jnp.arange(blocks, dtype=jnp.int32)
    )
    groups = queries.shape[0]
    asker_derivative = query_blocks.transpose(1, 0, 2, 3).reshape(groups, length, width)
    return (asker_derivative, key_acc[block_len:], value_acc[block_len:])


def body(queries, key_input, value_input, incoming, segments):
    shard_length = queries.shape[2]
    ctx_size = lax.axis_size("ctx")
    reach_dev = min(4, ctx_size - 1)
    block_len = reach_dev * shard_length
    scaling = 1.0 / math.sqrt(FEATURE_SIZE)
    doc_ids = segments[0]
    handed = passed_along(incoming, "pipe", -1)
    query_tok = queries[0, 0].reshape(shard_length, ASKER_STREAMS, FEATURE_SIZE)
    cot_tok = handed[0, 0].reshape(shard_length, ASKER_STREAMS, FEATURE_SIZE)
    key_widened = jnp.repeat(
        key_input[0, 0].reshape(shard_length, SHARED_GROUPS, FEATURE_SIZE), QUERY_PER_KEY, axis=1
    )
    value_widened = jnp.repeat(
        value_input[0, 0].reshape(shard_length, SHARED_GROUPS, FEATURE_SIZE), QUERY_PER_KEY, axis=1
    )
    query_head, key_head, value_head, cot_head = (
        lax.all_to_all(query_tok, "ctx", split_axis=1, concat_axis=0, tiled=True),
        lax.all_to_all(key_widened, "ctx", split_axis=1, concat_axis=0, tiled=True),
        lax.all_to_all(value_widened, "ctx", split_axis=1, concat_axis=0, tiled=True),
        lax.all_to_all(cot_tok, "ctx", split_axis=1, concat_axis=0, tiled=True),
    )

    def per_head(members):
        return banded(
            members[0][None], members[1], members[2], members[3][None], doc_ids, block_len, scaling
        )

    asker_derivative, lookup_derivative, content_derivative = lax.map(
        per_head,
        (
            query_head.transpose(1, 0, 2),
            key_head.transpose(1, 0, 2),
            value_head.transpose(1, 0, 2),
            cot_head.transpose(1, 0, 2),
        ),
    )
    asker_derivative = asker_derivative[:, 0].transpose(1, 0, 2)
    lookup_derivative = lookup_derivative.transpose(1, 0, 2)
    content_derivative = content_derivative.transpose(1, 0, 2)
    query_back, key_backward, value_backward = (
        lax.all_to_all(asker_derivative, "ctx", split_axis=0, concat_axis=1, tiled=True),
        lax.all_to_all(lookup_derivative, "ctx", split_axis=0, concat_axis=1, tiled=True),
        lax.all_to_all(content_derivative, "ctx", split_axis=0, concat_axis=1, tiled=True),
    )
    query_flat = query_back.reshape(shard_length, ASKER_STREAMS * FEATURE_SIZE)
    key_flattened = (
        key_backward.reshape(shard_length, SHARED_GROUPS, QUERY_PER_KEY, FEATURE_SIZE)
        .sum(axis=2)
        .reshape(shard_length, SHARED_GROUPS * FEATURE_SIZE)
    )
    value_flat = (
        value_backward.reshape(shard_length, SHARED_GROUPS, QUERY_PER_KEY, FEATURE_SIZE)
        .sum(axis=2)
        .reshape(shard_length, SHARED_GROUPS * FEATURE_SIZE)
    )
    offset_parts = jnp.concatenate(
        [jnp.sum(query_flat, axis=0), jnp.sum(key_flattened, axis=0), jnp.sum(value_flat, axis=0)]
    )
    offset_overall = lax.psum(offset_parts, ("ctx", "dp"))
    bias_scaled = offset_overall / math.sqrt(lax.axis_size("dp") * shard_length * ctx_size)
    query_grad = query_flat.astype(jnp.bfloat16)[None, None]
    key_grad = key_flattened.astype(jnp.bfloat16)[None, None]
    value_grad = value_flat.astype(jnp.bfloat16)[None, None]
    return (query_grad, key_grad, value_grad, bias_scaled[None])


def solution(mesh):
    return jax.shard_map(
        body,
        mesh=mesh,
        in_specs=(
            P("pipe", "dp", "ctx", None),
            P("pipe", "dp", "ctx", None),
            P("pipe", "dp", "ctx", None),
            P("pipe", "dp", "ctx", None),
            P("dp", None),
        ),
        out_specs=(
            P("pipe", "dp", "ctx", None),
            P("pipe", "dp", "ctx", None),
            P("pipe", "dp", "ctx", None),
            P("pipe", None),
        ),
        check_vma=False,
    )
```

profile of v0, /device:TPU:128, one launch (start us, length us, event | category | flops | bytes accessed | tf_op | source)
XLA Modules:
  0.0 1042.6 jit_solution(12610844461914456718)
XLA Ops:
  2.9 9.3 all-to-all-start.1
  12.2 28.5 %all-to-all-done.1 = bf16[128,32,128]{2,0,1:T(8,128)(2,1)S(1)} async-done(((bf16[128,32,128]{2,0,1:T(8,128)(2,1)}), bf16[128,32,128]{2,0,1:T(8,128)(2,1)S(1)}, u32[]{:S(2)}, u32[]{:S(2)}) %all-to-all-start.1) | async-done | bytes 1048608 | tf_op jit(solution)/shard_map/all_to_all | solution.py:113
  42.0 3.9 all-to-all-start.3
  47.8 37.3 %collective-permute-done = bf16[1,1,128,4096]{3,2,1,0:T(8,128)(2,1)S(1)} collective-permute-done((bf16[1,1,128,4096]{3,2,1,0:T(8,128)(2,1)}, bf16[1,1,128,4096]{3,2,1,0:T(8,128)(2,1)S(1)}, u32[]{:S(2)}, u32[]{:S(2)}) %collective-permute-start) | collective-permute-done | bytes 1048608 | tf_op jit(solution)/shard_map/ppermute | solution.py:16
  86.5 30.7 %all-to-all-start.2 = ((bf16[128,32,128]{0,2,1:T(8,128)(2,1)}), bf16[128,32,128]{0,2,1:T(8,128)(2,1)S(1)}, u32[]{:S(2)}, u32[]{:S(2)}) async-start(bf16[128,32,128]{0,2,1:T(8,128)(2,1)} %bitcast.112), calls=%async_computation.2 | async-start | bytes 2097152 | tf_op jit(solution)/shard_map/all_to_all | solution.py:115
  120.1 25.7 %all-to-all-done.2 = bf16[128,32,128]{0,2,1:T(8,128)(2,1)S(1)} async-done(((bf16[128,32,128]{0,2,1:T(8,128)(2,1)}), bf16[128,32,128]{0,2,1:T(8,128)(2,1)S(1)}, u32[]{:S(2)}, u32[]{:S(2)}) %all-to-all-start.2) | async-done | bytes 1048608 | tf_op jit(solution)/shard_map/all_to_all | solution.py:115
  145.8 4.7 all-to-all-start
  154.3 25.3 %all-to-all-done = bf16[128,32,128]{2,0,1:T(8,128)(2,1)} async-done(((bf16[128,32,128]{2,0,1:T(8,128)(2,1)}), bf16[128,32,128]{2,0,1:T(8,128)(2,1)}, u32[]{:S(2)}, u32[]{:S(2)}) %all-to-all-start) | async-done | bytes 1048608 | tf_op jit(solution)/shard_map/all_to_all | solution.py:112
  183.3 126.4 %while.25 = (s32[]{:T(128)}, f32[4608,128]{1,0:T(8,128)}, f32[4608,128]{1,0:T(8,128)}, f32[8,1,512,128]{3,2,1,0:T(8,128)}, s32[8]{0:T(128)}, /*index=5*/s32[4096...) while((s32[]{:T(128)}, f32[4608,128]{1,0:T(8,128)}, ...), condition=%wide.region_4.5_spmd, body=%wide.region_0.4_spmd.sunk | while | flops 820444160 | bytes 22487844 | solution.py:87
  192.3 2.4 fusion.59
  196.8 2.3 fusion.60
  208.1 2.4 fusion.59
  212.6 2.3 fusion.60
  223.9 2.4 fusion.59
  228.4 2.3 fusion.60
  239.7 2.4 fusion.59
  244.2 2.3 fusion.60
  255.5 2.4 fusion.59
  271.3 2.4 fusion.59
  275.8 2.3 fusion.60
  287.1 2.4 fusion.59
  291.6 2.3 fusion.60
  302.9 2.4 fusion.59
  307.4 2.3 fusion.60
  309.7 3.1 slice.8
  312.8 4.0 all-to-all-start.5
  316.8 3.1 slice.9
  319.9 48.6 %all-to-all-done.5 = f32[4096,1,128]{2,1,0:T(1,128)S(1)} async-done(((f32[4096,1,128]{2,1,0:T(1,128)}), f32[4096,1,128]{2,1,0:T(1,128)S(1)}, u32[]{:S(2)}, u32[]{:S(2)}) %all-to-all-start.5) | async-done | bytes 2097184 | tf_op jit(solution)/shard_map/all_to_all | solution.py:137
  368.5 56.4 %all_to_all.105 = f32[4096,1,128]{2,1,0:T(1,128)} all-to-all(f32[4096,1,128]{2,1,0:T(1,128)} %bitcast.109), channel_id=1, replica_groups=mesh['pipe'=4,'ctx'=32,'dp'=4] {'ctx'}, dimensions={0} | all-to-all | bytes 4194304 | tf_op jit(solution)/shard_map/all_to_all | solution.py:138
  424.9 4.8 all-to-all-start.4
  431.6 49.7 %all-to-all-done.4 = f32[4096,1,128]{2,1,0:T(1,128)} async-done(((f32[4096,1,128]{2,1,0:T(1,128)}), f32[4096,1,128]{2,1,0:T(1,128)}, u32[]{:S(2)}, u32[]{:S(2)}) %all-to-all-start.4) | async-done | bytes 2097184 | tf_op jit(solution)/shard_map/all_to_all | solution.py:136
  484.8 549.9 %psum.7 = f32[5120]{0:T(1024)S(1)} all-reduce(f32[5120]{0:T(1024)S(1)} %pad_maximum_fusion), channel_id=1, replica_groups=mesh['pipe'=4,'ctx'=32,'dp'=4] {'ctx','dp'}, use_global_device_ids=true, to_apply=%region_12.13 | all-reduce | flops 5120 | bytes 40960 | tf_op jit(solution)/shard_map/psum | solution.py:154
  (145 shorter events, 116.4 us)
Async XLA Ops:
  0.6 11.5 %copy-start = (bf16[1,1,128,512]{3,2,1,0:T(8,128)(2,1)S(1)}, bf16[1,1,128,512]{3,2,1,0:T(8,128)(2,1)}, u32[]{:S(2)}) copy-start(bf16[1,1,128,512]{3,2,1,0:T(8,128)(2,1)} %param.9) | copy-start | bytes 393220
  2.9 37.9 %all-to-all-start.1 = ((bf16[128,32,128]{2,0,1:T(8,128)(2,1)}), bf16[128,32,128]{2,0,1:T(8,128)(2,1)S(1)}, u32[]{:S(2)}, u32[]{:S(2)}) async-start(bf16[128,32,128]{2,0,1:T(8,128)(2,1)} %bitcast.9), calls=%async_computation.1 | async-start | bytes 2097152 | tf_op jit(solution)/shard_map/all_to_all | solution.py:113
  42.0 44.5 %all-to-all-start.3 = ((bf16[128,32,128]{2,0,1:T(8,128)(2,1)}), bf16[128,32,128]{2,0,1:T(8,128)(2,1)S(1)}, u32[]{:S(2)}, u32[]{:S(2)}) async-start(bf16[128,32,128]{2,0,1:T(8,128)(2,1)} %bitcast.17), calls=%async_computation.3 | async-start | bytes 2097152 | tf_op jit(solution)/shard_map/all_to_all | solution.py:114
  45.9 39.3 %collective-permute-start = (bf16[1,1,128,4096]{3,2,1,0:T(8,128)(2,1)}, bf16[1,1,128,4096]{3,2,1,0:T(8,128)(2,1)S(1)}, u32[]{:S(2)}, u32[]{:S(2)}) collective-permute-start(bf16[1,1,128,4096]{3,2,1,0:T(8,128)(2,1)} %param.10), channel_id=1, source_target_pairs={{0,384},{128,0},{256,128},{384,256},{1,385},{129,1},{257,129},{385... | collective-permute-start | bytes 3145736 | tf_op jit(solution)/shard_map/ppermute | solution.py:16
  86.5 59.3 %all-to-all-start.2 = ((bf16[128,32,128]{0,2,1:T(8,128)(2,1)}), bf16[128,32,128]{0,2,1:T(8,128)(2,1)S(1)}, u32[]{:S(2)}, u32[]{:S(2)}) async-start(bf16[128,32,128]{0,2,1:T(8,128)(2,1)} %bitcast.112), calls=%async_computation.2 | async-start | bytes 2097152 | tf_op jit(solution)/shard_map/all_to_all | solution.py:115
  118.7 31.8 %copy-start.1 = (s32[1,4096]{1,0:T(1,128)S(1)}, s32[1,4096]{1,0:T(1,128)}, u32[]{:S(2)}) copy-start(s32[1,4096]{1,0:T(1,128)} %param.11) | copy-start | bytes 49156
  145.8 33.8 %all-to-all-start = ((bf16[128,32,128]{2,0,1:T(8,128)(2,1)}), bf16[128,32,128]{2,0,1:T(8,128)(2,1)}, u32[]{:S(2)}, u32[]{:S(2)}) async-start(bf16[128,32,128]{2,0,1:T(8,128)(2,1)} %copy.41), calls=%async_computation | async-start | bytes 2097152 | tf_op jit(solution)/shard_map/all_to_all | solution.py:112
  312.8 55.7 %all-to-all-start.5 = ((f32[4096,1,128]{2,1,0:T(1,128)}), f32[4096,1,128]{2,1,0:T(1,128)S(1)}, u32[]{:S(2)}, u32[]{:S(2)}) async-start(f32[4096,1,128]{2,1,0:T(1,128)} %bitcast.108), calls=%async_computation.5 | async-start | bytes 4194304 | tf_op jit(solution)/shard_map/all_to_all | solution.py:137
  424.9 56.4 %all-to-all-start.4 = ((f32[4096,1,128]{2,1,0:T(1,128)}), f32[4096,1,128]{2,1,0:T(1,128)}, u32[]{:S(2)}, u32[]{:S(2)}) async-start(f32[4096,1,128]{2,1,0:T(1,128)} %bitcast.116), calls=%async_computation.4 | async-start | bytes 4194304 | tf_op jit(solution)/shard_map/all_to_all | solution.py:136
where the time goes:
time: 1050 us; the launch traced here: 1040 us
  blocking collectives  606 us (58%)
  waiting for transfers between devices  215 us (20%)
  matrix products  76.1 us (7%)
  starting transfers between devices  59.3 us (6%)
  local copies, waits for them, and re-layouts  57 us (5%)
  other arithmetic  23 us (2%)
    psum x1, blocking collectives, body(): offset_overall = lax.psum(offset_parts, ('ctx', 'dp'))  550 us
    all_to_all x1, blocking collectives, body(): lax.all_to_all(content_derivative, 'ctx', split_axis=0, concat_axis=1, ti...  56.4 us
    all_to_all x1, waiting for transfers between devices, body(): lax.all_to_all(asker_derivative, 'ctx', split_axis=0, concat_axis=1, tile...  49.7 us
    all_to_all x1, waiting for transfers between devices, body(): lax.all_to_all(lookup_derivative, 'ctx', split_axis=0, concat_axis=1, til...  48.6 us
    ppermute x1, waiting for transfers between devices, passed_along(): return lax.ppermute(value, axis, pairs)  37.3 us
    all_to_all x1, starting transfers between devices, body(): lax.all_to_all(cot_tok, 'ctx', split_axis=1, concat_axis=0, tiled=True)  30.7 us
    all_to_all x1, waiting for transfers between devices, body(): lax.all_to_all(key_widened, 'ctx', split_axis=1, concat_axis=0, tiled=True)  28.5 us
    all_to_all x1, waiting for transfers between devices, body(): lax.all_to_all(cot_tok, 'ctx', split_axis=1, concat_axis=0, tiled=True)  25.7 us
  transfers between devices with their start and end apart: 7, of which 6 were waited for; matrix products, arithmetic and copies ran while one was open for 1% of the time, Pallas kernels for 0%

commit v1 on v0

--- a/solution.py
+++ b/solution.py
@@ -8,6 +8,12 @@
 SHARED_GROUPS = 4
 FEATURE_SIZE = 128
 QUERY_PER_KEY = 8
+
+
+def swap_blocks(x, mesh_axis, split, join):
+    parts = jnp.split(x, lax.axis_size(mesh_axis), axis=split)
+    received = lax.all_to_all(jnp.stack(parts), mesh_axis, 0, 0)
+    return jnp.concatenate(received, axis=join)
 
 
 def passed_along(value, axis, steps):
@@ -109,7 +115,7 @@
         value_input[0, 0].reshape(shard_length, SHARED_GROUPS, FEATURE_SIZE), QUERY_PER_KEY, axis=1
     )
     query_head, key_head, value_head, cot_head = (
-        lax.all_to_all(query_tok, "ctx", split_axis=1, concat_axis=0, tiled=True),
+        swap_blocks(query_tok, "ctx", 1, 0),
         lax.all_to_all(key_widened, "ctx", split_axis=1, concat_axis=0, tiled=True),
         lax.all_to_all(value_widened, "ctx", split_axis=1, concat_axis=0, tiled=True),
         lax.all_to_all(cot_tok, "ctx", split_axis=1, concat_axis=0, tiled=True),

time: 1050 us -> 1040 us (level)
  the two profiles are of different devices: /device:TPU:128 before, /device:TPU:32 now
where the time goes in v1:
time: 1040 us; the launch traced here: 1030 us
  blocking collectives  613 us (59%)
  waiting for transfers between devices  173 us (17%)
  local copies, waits for them, and re-layouts  79.3 us (8%)
  matrix products  76.1 us (7%)
  starting transfers between devices  63.4 us (6%)
  other arithmetic  23 us (2%)
    psum x1, blocking collectives, body(): offset_overall = lax.psum(offset_parts, ('ctx', 'dp'))  554 us
    all_to_all x1, blocking collectives, body(): lax.all_to_all(content_derivative, 'ctx', split_axis=0, concat_axis=1, ti...  58.2 us
    all_to_all x1, waiting for transfers between devices, body(): lax.all_to_all(asker_derivative, 'ctx', split_axis=0, concat_axis=1, tile...  43.2 us
    all_to_all x1, waiting for transfers between devices, body(): lax.all_to_all(lookup_derivative, 'ctx', split_axis=0, concat_axis=1, til...  42 us
    all_to_all x1, waiting for transfers between devices, body(): lax.all_to_all(key_widened, 'ctx', split_axis=1, concat_axis=0, tiled=True)  36.3 us
    unnamed x41, local copies, waits for them, and re-layouts  23.6 us
  transfers between devices with their start and end apart: 7, of which 6 were waited for; matrix products, arithmetic and copies ran while one was open for 4% of the time, Pallas kernels for 0%

profile of v1, /device:TPU:32, one launch (start us, length us, event | category | flops | bytes accessed | tf_op | source)
XLA Modules:
  0.0 1033.0 jit_solution(4003555196971483441)
XLA Ops:
  0.6 11.1 %collective-permute-start = (bf16[1,1,128,4096]{3,2,1,0:T(8,128)(2,1)}, bf16[1,1,128,4096]{3,2,1,0:T(8,128)(2,1)}, u32[]{:S(2)}, u32[]{:S(2)}) collective-permute-start(bf16[1,1,128,4096]{3,2,1,0:T(8,128)(2,1)} %param.10), channel_id=1, source_target_pairs={{0,384},{128,0},{256,128},{384,256},{1,385},{129,1},{257,129},{385... | collective-permute-start | bytes 3145736 | tf_op jit(solution)/shard_map/ppermute | solution.py:22
  14.0 8.4 all-to-all-start.1
  30.5 36.3 %all-to-all-done.1 = bf16[128,32,128]{2,0,1:T(8,128)(2,1)S(1)} async-done(((bf16[128,32,128]{2,0,1:T(8,128)(2,1)}), bf16[128,32,128]{2,0,1:T(8,128)(2,1)S(1)}, u32[]{:S(2)}, u32[]{:S(2)}) %all-to-all-start.1) | async-done | bytes 1048608 | tf_op jit(solution)/shard_map/all_to_all | solution.py:119
  68.0 7.4 all-to-all-start.3
  83.9 15.7 %all-to-all-done.3 = bf16[128,32,128]{2,0,1:T(8,128)(2,1)S(1)} async-done(((bf16[128,32,128]{2,0,1:T(8,128)(2,1)}), bf16[128,32,128]{2,0,1:T(8,128)(2,1)S(1)}, u32[]{:S(2)}, u32[]{:S(2)}) %all-to-all-start.3) | async-done | bytes 1048608 | tf_op jit(solution)/shard_map/all_to_all | solution.py:120
  99.6 9.0 all-to-all-start.2
  117.0 16.0 %all-to-all-done.2 = bf16[128,32,128]{0,2,1:T(8,128)(2,1)} async-done(((bf16[128,32,128]{0,2,1:T(8,128)(2,1)}), bf16[128,32,128]{0,2,1:T(8,128)(2,1)}, u32[]{:S(2)}, u32[]{:S(2)}) %all-to-all-start.2) | async-done | bytes 1048608 | tf_op jit(solution)/shard_map/all_to_all | solution.py:121
  133.0 9.4 all-to-all-start
  147.2 19.7 %all-to-all-done = bf16[32,128,1,128]{3,1,2,0:T(8,128)(2,1)} async-done(((bf16[32,128,1,128]{3,1,2,0:T(8,128)(2,1)}), bf16[32,128,1,128]{3,1,2,0:T(8,128)(2,1)}, u32[]{:S(2)}, u32[]{:S(2)}) %all-to-all-start) | async-done | bytes 1048608 | tf_op jit(solution)/shard_map/all_to_all | solution.py:15
  170.6 126.8 %while.25 = (s32[]{:T(128)}, f32[4608,128]{1,0:T(8,128)}, f32[4608,128]{1,0:T(8,128)}, f32[8,1,512,128]{3,2,1,0:T(8,128)}, s32[8]{0:T(128)}, /*index=5*/s32[4096...) while((s32[]{:T(128)}, f32[4608,128]{1,0:T(8,128)}, ...), condition=%wide.region_4.5_spmd, body=%wide.region_0.4_spmd.sunk | while | flops 820444160 | bytes 22487844 | solution.py:93
  179.7 2.4 fusion.59
  184.1 2.3 fusion.60
  195.5 2.4 fusion.59
  200.0 2.3 fusion.60
  211.3 2.4 fusion.59
  215.8 2.3 fusion.60
  227.2 2.4 fusion.59
  231.7 2.3 fusion.60
  243.1 2.4 fusion.59
  258.9 2.4 fusion.59
  263.4 2.3 fusion.60
  274.8 2.4 fusion.59
  279.3 2.3 fusion.60
  290.6 2.4 fusion.59
  297.5 3.1 slice.8
  300.6 8.8 all-to-all-start.5
  309.4 3.1 slice.9
  312.4 42.0 %all-to-all-done.5 = f32[4096,1,128]{2,1,0:T(1,128)S(1)} async-done(((f32[4096,1,128]{2,1,0:T(1,128)}), f32[4096,1,128]{2,1,0:T(1,128)S(1)}, u32[]{:S(2)}, u32[]{:S(2)}) %all-to-all-start.5) | async-done | bytes 2097184 | tf_op jit(solution)/shard_map/all_to_all | solution.py:143
  354.4 58.2 %all_to_all.95 = f32[4096,1,128]{2,1,0:T(1,128)} all-to-all(f32[4096,1,128]{2,1,0:T(1,128)} %bitcast.230), channel_id=1, replica_groups=mesh['pipe'=4,'ctx'=32,'dp'=4] {'ctx'}, dimensions={0} | all-to-all | bytes 4194304 | tf_op jit(solution)/shard_map/all_to_all | solution.py:144
  412.7 9.5 all-to-all-start.4
  424.1 43.2 %all-to-all-done.4 = f32[4096,1,128]{2,1,0:T(1,128)} async-done(((f32[4096,1,128]{2,1,0:T(1,128)}), f32[4096,1,128]{2,1,0:T(1,128)}, u32[]{:S(2)}, u32[]{:S(2)}) %all-to-all-start.4) | async-done | bytes 2097184 | tf_op jit(solution)/shard_map/all_to_all | solution.py:142
  470.8 554.4 %psum.7 = f32[5120]{0:T(1024)S(1)} all-reduce(f32[5120]{0:T(1024)S(1)} %pad_maximum_fusion), channel_id=1, replica_groups=mesh['pipe'=4,'ctx'=32,'dp'=4] {'ctx','dp'}, use_global_device_ids=true, to_apply=%region_12.13 | all-reduce | flops 5120 | bytes 40960 | tf_op jit(solution)/shard_map/psum | solution.py:160
  (179 shorter events, 139.1 us)
Async XLA Ops:
  0.6 21.8 %copy-start = (bf16[1,1,128,4096]{3,2,1,0:T(8,128)(2,1)S(1)}, bf16[1,1,128,4096]{3,2,1,0:T(8,128)(2,1)}, u32[]{:S(2)}) copy-start(bf16[1,1,128,4096]{3,2,1,0:T(8,128)(2,1)} %param.7) | copy-start | bytes 3145732
  0.6 80.9 %collective-permute-start = (bf16[1,1,128,4096]{3,2,1,0:T(8,128)(2,1)}, bf16[1,1,128,4096]{3,2,1,0:T(8,128)(2,1)}, u32[]{:S(2)}, u32[]{:S(2)}) collective-permute-start(bf16[1,1,128,4096]{3,2,1,0:T(8,128)(2,1)} %param.10), channel_id=1, source_target_pairs={{0,384},{128,0},{256,128},{384,256},{1,385},{129,1},{257,129},{385... | collective-permute-start | bytes 3145736 | tf_op jit(solution)/shard_map/ppermute | solution.py:22
  14.0 11.0 %copy-start.1 = (bf16[1,1,128,512]{3,2,1,0:T(8,128)(2,1)S(1)}, bf16[1,1,128,512]{3,2,1,0:T(8,128)(2,1)}, u32[]{:S(2)}) copy-start(bf16[1,1,128,512]{3,2,1,0:T(8,128)(2,1)} %param.9) | copy-start | bytes 393220
  14.0 52.8 %all-to-all-start.1 = ((bf16[128,32,128]{2,0,1:T(8,128)(2,1)}), bf16[128,32,128]{2,0,1:T(8,128)(2,1)S(1)}, u32[]{:S(2)}, u32[]{:S(2)}) async-start(bf16[128,32,128]{2,0,1:T(8,128)(2,1)} %bitcast.40), calls=%async_computation.1 | async-start | bytes 2097152 | tf_op jit(solution)/shard_map/all_to_all | solution.py:119
  68.0 31.6 %all-to-all-start.3 = ((bf16[128,32,128]{2,0,1:T(8,128)(2,1)}), bf16[128,32,128]{2,0,1:T(8,128)(2,1)S(1)}, u32[]{:S(2)}, u32[]{:S(2)}) async-start(bf16[128,32,128]{2,0,1:T(8,128)(2,1)} %bitcast.266), calls=%async_computation.3 | async-start | bytes 2097152 | tf_op jit(solution)/shard_map/all_to_all | solution.py:120
  99.6 33.5 %all-to-all-start.2 = ((bf16[128,32,128]{0,2,1:T(8,128)(2,1)}), bf16[128,32,128]{0,2,1:T(8,128)(2,1)}, u32[]{:S(2)}, u32[]{:S(2)}) async-start(bf16[128,32,128]{0,2,1:T(8,128)(2,1)} %bitcast.265), calls=%async_computation.2 | async-start | bytes 2097152 | tf_op jit(solution)/shard_map/all_to_all | solution.py:121
  114.7 27.7 %copy-start.2 = (s32[1,4096]{1,0:T(1,128)S(1)}, s32[1,4096]{1,0:T(1,128)}, u32[]{:S(2)}) copy-start(s32[1,4096]{1,0:T(1,128)} %param.11) | copy-start | bytes 49156
  133.0 33.8 %all-to-all-start = ((bf16[32,128,1,128]{3,1,2,0:T(8,128)(2,1)}), bf16[32,128,1,128]{3,1,2,0:T(8,128)(2,1)}, u32[]{:S(2)}, u32[]{:S(2)}) async-start(bf16[32,128,1,128]{3,1,2,0:T(8,128)(2,1)} %copy.135), calls=%async_computation | async-start | bytes 2097152 | tf_op jit(solution)/shard_map/all_to_all | solution.py:15
  300.6 53.9 %all-to-all-start.5 = ((f32[4096,1,128]{2,1,0:T(1,128)}), f32[4096,1,128]{2,1,0:T(1,128)S(1)}, u32[]{:S(2)}, u32[]{:S(2)}) async-start(f32[4096,1,128]{2,1,0:T(1,128)} %bitcast.229), calls=%async_computation.5 | async-start | bytes 4194304 | tf_op jit(solution)/shard_map/all_to_all | solution.py:143
  412.7 54.6 %all-to-all-start.4 = ((f32[4096,1,128]{2,1,0:T(1,128)}), f32[4096,1,128]{2,1,0:T(1,128)}, u32[]{:S(2)}, u32[]{:S(2)}) async-start(f32[4096,1,128]{2,1,0:T(1,128)} %bitcast.269), calls=%async_computation.4 | async-start | bytes 4194304 | tf_op jit(solution)/shard_map/all_to_all | solution.py:142
